TPU v7x, 128 devices: a whole 4x4x4 slice. The times are simulated.
128 devices in a mesh: seq: 64 (over z, x, y_lo, core), chan: 2 (over y_hi).
Axes of the slice: x: 4, y: 4 (y_hi: 2, y_lo: 2; y = y_hi * 2 + y_lo), z: 4, core: 2. Of those that a mesh axis runs over, the one named last changes fastest.
Arguments:
- signal: bfloat16 [2, 32768, 128], P('chan', 'seq'), may hold values from -6 to 6
- cotangent: bfloat16 [2, 32768, 128], P('chan', 'seq'), may hold values from -6 to 6
- band_freq: int32 [16], replicated, may hold values from 1 to 8191
- w_embed: float32 [32, 64], replicated, may hold values from -2 to 2
- b_embed: float32 [64], replicated, may hold values from -3.140625 to 3.140625
- w_out: float32 [64, 128], P(None, 'chan'), may hold values from -0.75 to 0.75
- decay: float32 [128], P('chan'), may hold values from 0.25 to 16, as said below
Outputs:
- conv_out: bfloat16 [2, 32768, 128], P('chan', 'seq')
- d_signal: bfloat16 [2, 32768, 128], P('chan', 'seq')
- grad_embed: float32 [32, 64], replicated
- grad_bias: float32 [64], replicated
- grad_out: float32 [64, 128], P(None, 'chan')
Inputs may be any that keep to these rules, and one draw needn't show every extreme that they name: decay rates are positive.
All inputs are finite; a program needn't handle non-finite values.
Results may differ from a plain program's by a relative error of at most 0.007.
Values may be sent and summed in bfloat16 or wider, within the bound.
No kernel may reach another device: no remote copies, remote signals or barrier semaphores. Data moves between devices by JAX's collectives and lax.ppermute only.
A program may use at most 192 MiB of HBM per device.

v0:
```python
import math
import jax
import jax.numpy as jnp
from jax import lax
from jax.sharding import PartitionSpec as P

exact_mode = lax.Precision.HIGHEST


def mat_dot(lhs_mat, rhs_mat):
    return jnp.dot(lhs_mat, rhs_mat, preferred_element_type=jnp.float32, precision=exact_mode)


def side_dot(table, values):
    return jnp.einsum(
        "db,cbm->cdm", table, values, preferred_element_type=jnp.float32, precision=exact_mode
    )


def inner_dot(table, values):
    return jnp.einsum(
        "eb,cdbh->cdeh", table, values, preferred_element_type=jnp.float32, precision=exact_mode
    )


def band_phase(band_freq, places, seq_total):
    upper_part = places // 1024
    lower_part = places % 1024
    partial_turn = upper_part[:, None] * band_freq[None, :] % seq_total
    wrapped = (partial_turn * 1024 + lower_part[:, None] * band_freq[None, :]) % seq_total
    return wrapped.astype(jnp.float32) * (2.0 * math.pi / seq_total)


def filter_parts(places, band_freq, w_embed, b_embed, w_out, decay, seq_total):
    phases = band_phase(band_freq, places, seq_total)
    features = jnp.concatenate([jnp.cos(phases), jnp.sin(phases)], axis=1)
    preact = mat_dot(features, w_embed) + b_embed[None, :]
    hidden = jnp.sin(preact)
    fraction = places.astype(jnp.float32) / seq_total
    envelope = (
        jnp.exp(-decay[None, :] * fraction[:, None]) * jnp.sqrt((1.0 + decay) / seq_total)[None, :]
    )
    taps = mat_dot(hidden, w_out) * envelope
    return (features, preact, hidden, taps, envelope)


def angle_table(rows_idx, cols_idx, modulus):
    wrapped = rows_idx[:, None] * cols_idx[None, :] % modulus
    angles = wrapped.astype(jnp.float32) * (2.0 * math.pi / modulus)
    return (jnp.cos(angles), jnp.sin(angles))


def local(signal, cotangent, band_freq, w_embed, b_embed, w_out, decay):
    devices = lax.axis_size("seq")
    rank_seq = lax.axis_index("seq")
    seg_len = signal.shape[1] * 2
    channels = signal.shape[2] // 2
    block_w = seg_len // devices
    rows_all = 2 * devices
    seq_total = seg_len * devices
    fft_size = 2 * seq_total
    inv_scale = 1.0 / fft_size
    radix_one = max(
        (divisor for divisor in range(1, math.isqrt(seg_len) + 1) if seg_len % divisor == 0)
    )
    radix_two = seg_len // radix_one
    row_ids = jnp.arange(rows_all, dtype=jnp.int32)
    src_ids = jnp.arange(devices, dtype=jnp.int32)
    col_glob = rank_seq * block_w + jnp.arange(block_w, dtype=jnp.int32)
    seg_ids = jnp.arange(seg_len, dtype=jnp.int32)
    one_ids = jnp.arange(radix_one, dtype=jnp.int32)
    two_ids = jnp.arange(radix_two, dtype=jnp.int32)
    pair_ids = lax.dynamic_slice_in_dim(row_ids, 2 * rank_seq, 2)
    outer_cos, outer_sin = angle_table(row_ids, src_ids, rows_all)
    entry_cos, entry_sin = angle_table(row_ids, col_glob, fft_size)
    first_cos, first_sin = angle_table(one_ids, one_ids, radix_one)
    second_cos, second_sin = angle_table(two_ids, two_ids, radix_two)
    inner_cos, inner_sin = angle_table(one_ids, two_ids, seg_len)
    exit_cos, exit_sin = angle_table(pair_ids, seg_ids, fft_size)
    inner_c = inner_cos[None, :, :, None]
    inner_s = inner_sin[None, :, :, None]

    def twist_stack(real_a, imag_a):
        real_a = real_a.reshape(rows_all, block_w, channels)
        imag_a = imag_a.reshape(rows_all, block_w, channels)
        twist_c = entry_cos[:, :, None]
        twist_s = entry_sin[:, :, None]
        real_b = real_a * twist_c + imag_a * twist_s
        imag_b = imag_a * twist_c - real_a * twist_s
        return jnp.stack([real_b, imag_b]).reshape(2, rows_all, block_w * channels)

    def column_pass(cols_data):
        return twist_stack(mat_dot(outer_cos, cols_data), -mat_dot(outer_sin, cols_data))

    def local_forward(stacked):
        grid = stacked.reshape(2, 2, radix_one, radix_two * channels)
        part_r = side_dot(first_cos, grid[0]) + side_dot(first_sin, grid[1])
        part_i = side_dot(first_cos, grid[1]) - side_dot(first_sin, grid[0])
        part_r = part_r.reshape(2, radix_one, radix_two, channels)
        part_i = part_i.reshape(2, radix_one, radix_two, channels)
        turn_r = part_r * inner_c + part_i * inner_s
        turn_i = part_i * inner_c - part_r * inner_s
        spec_r = inner_dot(second_cos, turn_r) + inner_dot(second_sin, turn_i)
        spec_i = inner_dot(second_cos, turn_i) - inner_dot(second_sin, turn_r)
        return (spec_r, spec_i)

    def local_inverse(spec_r, spec_i):
        back_r = inner_dot(second_cos, spec_r) - inner_dot(second_sin, spec_i)
        back_i = inner_dot(second_cos, spec_i) + inner_dot(second_sin, spec_r)
        turn_r = (back_r * inner_c - back_i * inner_s).reshape(2, radix_one, radix_two * channels)
        turn_i = (back_r * inner_s + back_i * inner_c).reshape(2, radix_one, radix_two * channels)
        time_r = (side_dot(first_cos, turn_r) - side_dot(first_sin, turn_i)).reshape(
            2, seg_len, channels
        )
        time_i = (side_dot(first_cos, turn_i) + side_dot(first_sin, turn_r)).reshape(
            2, seg_len, channels
        )
        twist_c = exit_cos[:, :, None]
        twist_s = exit_sin[:, :, None]
        final_r = time_r * twist_c - time_i * twist_s
        final_i = time_r * twist_s + time_i * twist_c
        return jnp.stack([final_r, final_i]).reshape(2, 2, seg_len * channels)

    def real_rows(gathered):
        return mat_dot(outer_cos.T, gathered[0]) - mat_dot(outer_sin.T, gathered[1])

    sig_cols, cot_cols = (
        lax.all_to_all(
            signal.reshape(devices, block_w * channels),
            "seq",
            split_axis=0,
            concat_axis=0,
            tiled=True,
        ),
        lax.all_to_all(
            cotangent.reshape(devices, block_w * channels),
            "seq",
            split_axis=0,
            concat_axis=0,
            tiled=True,
        ),
    )
    places = rank_seq * seg_len + seg_ids
    features, preact, hidden, taps, envelope = filter_parts(
        places, band_freq, w_embed, b_embed, w_out, decay, seq_total
    )
    tap_cols = lax.all_to_all(
        taps.reshape(devices, block_w * channels), "seq", split_axis=0, concat_axis=0, tiled=True
    )
    spec_sig, spec_cot, spec_tap = (
        lax.all_to_all(
            column_pass(sig_cols.astype(jnp.float32)),
            "seq",
            split_axis=1,
            concat_axis=2,
            tiled=True,
        ),
        lax.all_to_all(
            column_pass(cot_cols.astype(jnp.float32)),
            "seq",
            split_axis=1,
            concat_axis=2,
            tiled=True,
        ),
        lax.all_to_all(column_pass(tap_cols), "seq", split_axis=1, concat_axis=2, tiled=True),
    )
    sig_r, sig_i = local_forward(spec_sig)
    cot_r, cot_i = local_forward(spec_cot)
    tap_r, tap_i = local_forward(spec_tap)
    prod_r = sig_r * tap_r - sig_i * tap_i
    prod_i = sig_r * tap_i + sig_i * tap_r
    grad_r = cot_r * tap_r + cot_i * tap_i
    grad_i = cot_i * tap_r - cot_r * tap_i
    corr_r = cot_r * sig_r + cot_i * sig_i
    corr_i = cot_i * sig_r - cot_r * sig_i
    prod_back, grad_back, corr_back = (
        lax.all_to_all(
            local_inverse(prod_r, prod_i), "seq", split_axis=2, concat_axis=1, tiled=True
        ),
        lax.all_to_all(
            local_inverse(grad_r, grad_i), "seq", split_axis=2, concat_axis=1, tiled=True
        ),
        lax.all_to_all(
            local_inverse(corr_r, corr_i), "seq", split_axis=2, concat_axis=1, tiled=True
        ),
    )
    out_cols = real_rows(prod_back)
    dsig_cols = real_rows(grad_back)
    dtap_cols = real_rows(corr_back) * inv_scale
    out_rows, dsig_rows = (
        lax.all_to_all(
            (out_cols * inv_scale).astype(jnp.bfloat16),
            "seq",
            split_axis=0,
            concat_axis=0,
            tiled=True,
        ),
        lax.all_to_all(
            (dsig_cols * inv_scale).astype(jnp.bfloat16),
            "seq",
            split_axis=0,
            concat_axis=0,
            tiled=True,
        ),
    )
    conv_out = out_rows.reshape(1, seg_len // 2, 2 * channels)
    d_signal = dsig_rows.reshape(1, seg_len // 2, 2 * channels)
    d_taps = (
        lax.all_to_all(
            dtap_cols.astype(jnp.bfloat16), "seq", split_axis=0, concat_axis=0, tiled=True
        )
        .astype(dtap_cols.dtype)
        .reshape(seg_len, channels)
    )
    d_raw = d_taps * envelope
    d_preact = mat_dot(d_raw, w_out.T) * jnp.cos(preact)
    out_part = mat_dot(hidden.T, d_raw)
    embed_part = mat_dot(features.T, d_preact)
    bias_part = jnp.sum(d_preact, axis=0)
    out_sum, embed_sum, bias_sum = lax.psum((out_part, embed_part, bias_part), "seq")
    embed_all, bias_all = lax.psum((embed_sum, bias_sum), "chan")
    norm_scale = 1.0 / math.sqrt(seq_total)
    return (conv_out, d_signal, embed_all * norm_scale, bias_all * norm_scale, out_sum * norm_scale)


def solution(mesh):
    return jax.shard_map(
        local,
        mesh=mesh,
        in_specs=(
            P("chan", "seq", None),
            P("chan", "seq", None),
            P(),
            P(),
            P(),
            P(None, "chan"),
            P("chan"),
        ),
        out_specs=(P("chan", "seq", None), P("chan", "seq", None), P(), P(), P(None, "chan")),
        check_vma=False,
    )
```

profile of v0, /device:TPU:0, one launch (start us, length us, event | category | flops | bytes accessed | tf_op | source)
XLA Modules:
  0.0 1673.4 jit_solution(10459679201133411678)
XLA Ops:
  4.5 9.9 all-to-all-start
  19.5 2.7 fusion.489
  24.7 8.8 all-to-all-start.6
  34.2 7.9 all-to-all-done.6
  42.1 5.1 all-to-all-start.2
  49.2 7.9 all-to-all-done.2
  59.8 3.0 multiply_add_fusion.8
  65.5 1.9 pad_maximum_fusion.1
  67.4 4.7 all-to-all-start.3
  79.9 2.0 pad_maximum_fusion.3
  81.9 3.0 pad_maximum_fusion
  84.9 5.3 all-to-all-done.3
  90.2 4.7 all-to-all-start.1
  94.9 1.6 fusion.486
  101.8 11.2 all-to-all-done.1
  113.0 5.7 all-to-all-start.7
  123.7 2.3 fusion.40
  126.0 2.5 fusion.3
  129.9 2.8 reshape.612
  132.7 2.3 fusion.39
  135.0 3.5 fusion.42
  138.5 3.5 fusion.41
  142.0 3.8 fusion.484
  146.8 2.0 squeeze.48
  148.9 2.5 fusion.132
  151.4 2.0 copy.97
  153.4 2.0 squeeze.49
  155.5 1.7 fusion.130
  157.2 2.7 fusion.6
  159.9 2.5 fusion.7
  167.9 2.8 convolution_subtract_fusion.11
  170.7 2.8 convolution_add_fusion.11
  173.6 3.1 convolution_subtract_fusion.10
  176.7 3.6 convolution_add_fusion.10
  181.6 1.9 multiply_add_fusion
  195.8 3.3 subtract_bitcast_fusion
  222.6 1.9 reshape.630
  224.5 3.6 multiply_subtract_fusion.6
  228.6 58.0 %copy.88 = f32[2,2,65536]{1,0,2:T(2,128)} copy(f32[2,2,65536]{2,1,0:T(2,128)S(1)} %pad_maximum_fusion.2) | data formatting | bytes 2097152 | tf_op jit(solution)/shard_map/stack | solution.py:122
  286.6 96.8 %reshape.642 = f32[64,1,4096]{2,1,0:T(1,128)} reshape(f32[65536,2,2]{2,1,0:T(2,128)} %bitcast.255) | data formatting | bytes 2097152
  383.4 8.7 all-to-all-start.4
  392.7 58.0 %copy.98 = f32[2,2,65536]{1,0,2:T(2,128)} copy(f32[2,2,65536]{2,1,0:T(2,128)S(1)} %pad_maximum_fusion.4) | data formatting | bytes 2097152 | tf_op jit(solution)/shard_map/stack | solution.py:122
  450.7 96.8 %reshape.648 = f32[64,1,4096]{2,1,0:T(1,128)} reshape(f32[65536,2,2]{2,1,0:T(2,128)} %bitcast.257) | data formatting | bytes 2097152
  547.5 8.8 all-to-all-start.8
  556.3 1.7 pad_maximum_fusion.5
  558.0 58.0 %copy.101 = f32[2,2,65536]{1,0,2:T(2,128)} copy(f32[2,2,65536]{2,1,0:T(2,128)S(1)} %pad_maximum_fusion.5) | data formatting | bytes 2097152 | tf_op jit(solution)/shard_map/stack | solution.py:122
  616.0 96.8 %reshape.652 = f32[64,1,4096]{2,1,0:T(1,128)} reshape(f32[65536,2,2]{2,1,0:T(2,128)} %bitcast.259) | data formatting | bytes 2097152
  713.3 3.3 reduce.6
  716.5 129.2 %reshape.643 = f32[65536,2,2]{2,1,0:T(2,128)} reshape(f32[64,4096]{1,0:T(8,128)S(1)} %reduce.6) | data formatting | bytes 2097152
  845.8 71.0 %copy.89 = f32[2,2,64,1024]{3,1,2,0:T(2,128)S(1)} copy(f32[2,2,64,1024]{1,0,3,2:T(2,128)} %bitcast.35) | data formatting | bytes 2097152 | tf_op jit(solution)/shard_map/all_to_all | solution.py:177
  917.6 9.1 all-to-all-start.10
  929.1 3.3 reduce.8
  932.4 129.0 %reshape.649 = f32[65536,2,2]{2,1,0:T(2,128)} reshape(f32[64,4096]{1,0:T(8,128)S(1)} %reduce.8) | data formatting | bytes 2097152
  1061.4 71.0 %copy.99 = f32[2,2,64,1024]{3,1,2,0:T(2,128)S(1)} copy(f32[2,2,64,1024]{1,0,3,2:T(2,128)} %bitcast.54) | data formatting | bytes 2097152 | tf_op jit(solution)/shard_map/all_to_all | solution.py:180
  1135.7 9.4 all-to-all-start.5
  1145.1 3.3 reduce.10
  1148.4 129.0 %reshape.653 = f32[65536,2,2]{2,1,0:T(2,128)} reshape(f32[64,4096]{1,0:T(8,128)S(1)} %reduce.10) | data formatting | bytes 2097152
  1277.5 71.0 %copy.102 = f32[2,2,64,1024]{3,1,2,0:T(2,128)S(1)} copy(f32[2,2,64,1024]{1,0,3,2:T(2,128)} %bitcast.63) | data formatting | bytes 2097152 | tf_op jit(solution)/shard_map/all_to_all | solution.py:183
  1349.8 9.1 all-to-all-start.9
  1360.9 6.4 all-to-all-done.9
  1367.4 4.6 all-to-all-start.11
  1375.1 5.4 all-to-all-done.11
  1383.9 276.3 %all-reduce = (f32[32,64]{1,0:T(8,128)S(1)}, f32[64]{0:T(128)S(1)}, f32[64,64]{1,0:T(8,128)S(1)}) all-reduce(f32[32,64]{1,0:T(8,128)S(1)} %fusion.61, f32[64]{0:T(128)S(1)} %get-tuple-element.72, f32[64,64]{1,0:T(8,128)S(1)} %fusion.48), channel_id=1, replica_groups=mesh['seq'=64,'chan'=2] {'seq'}, use_global_device_ids=true, to_apply=%region_0.1 | all-reduce | flops 6208 | bytes 49664 | tf_op jit(solution)/shard_map/psum | solution.py:220
  1660.2 11.2 all-reduce.1
  (184 shorter events, 101.6 us)
Async XLA Ops:
  0.6 22.3 %copy-start = (f32[64,64]{1,0:T(8,128)S(1)}, f32[64,64]{1,0:T(8,128)}, u32[]{:S(2)}) copy-start(f32[64,64]{1,0:T(8,128)} %param.12) | copy-start | bytes 49156
  4.5 20.2 %all-to-all-start = ((bf16[64,2,512]{2,1,0:T(2,128)(2,1)}), bf16[64,2,512]{2,1,0:T(2,128)(2,1)S(1)}, u32[]{:S(2)}, u32[]{:S(2)}) async-start(bf16[64,2,512]{2,1,0:T(2,128)(2,1)} %reshape.640), calls=%async_computation | async-start | bytes 262144 | tf_op jit(solution)/shard_map/all_to_all | solution.py:128
  14.4 7.8 copy-start.12
  15.1 7.1 copy-start.14
  15.1 7.1 copy-start.16
  19.5 2.7 copy-start.8
  19.5 2.7 copy-start.10
  22.2 0.7 copy-start.3
  24.7 17.4 %all-to-all-start.6 = ((bf16[64,2,512]{2,1,0:T(2,128)(2,1)}), bf16[64,2,512]{2,1,0:T(2,128)(2,1)S(1)}, u32[]{:S(2)}, u32[]{:S(2)}) async-start(bf16[64,2,512]{2,1,0:T(2,128)(2,1)} %reshape.646), calls=%async_computation.6 | async-start | bytes 262144 | tf_op jit(solution)/shard_map/all_to_all | solution.py:135
  42.1 15.0 all-to-all-start.2
  67.4 22.7 %all-to-all-start.3 = ((f32[2,128,1024]{2,0,1:T(2,128)}), f32[2,128,1024]{2,0,1:T(2,128)S(1)}, u32[]{:S(2)}, u32[]{:S(2)}) async-start(f32[2,128,1024]{2,0,1:T(2,128)} %pad_maximum_fusion.1), calls=%async_computation.3 | async-start | bytes 2097152 | tf_op jit(solution)/shard_map/all_to_all | solution.py:165
  90.2 22.8 %all-to-all-start.1 = ((f32[2,128,1024]{2,0,1:T(2,128)}), f32[2,128,1024]{2,0,1:T(2,128)S(1)}, u32[]{:S(2)}, u32[]{:S(2)}) async-start(f32[2,128,1024]{2,0,1:T(2,128)} %pad_maximum_fusion), calls=%async_computation.1 | async-start | bytes 2097152 | tf_op jit(solution)/shard_map/all_to_all | solution.py:151
  113.0 29.0 %all-to-all-start.7 = ((f32[2,128,1024]{2,0,1:T(2,128)}), f32[2,128,1024]{2,0,1:T(2,128)}, u32[]{:S(2)}, u32[]{:S(2)}) async-start(f32[2,128,1024]{2,0,1:T(2,128)} %pad_maximum_fusion.3), calls=%async_computation.7 | async-start | bytes 2097152 | tf_op jit(solution)/shard_map/all_to_all | solution.py:158
  123.7 36.2 %copy-start.1 = (f32[2,32,32,64]{3,2,1,0:T(8,128)}, f32[2,32,32,64]{3,2,1,0:T(8,128)S(1)}, u32[]{:S(2)}) copy-start(f32[2,32,32,64]{3,2,1,0:T(8,128)S(1)} %reshape.610) | copy-start | bytes 1572868
  129.9 32.5 %copy-start.2 = (f32[2,32,32,64]{3,2,1,0:T(8,128)}, f32[2,32,32,64]{3,2,1,0:T(8,128)S(1)}, u32[]{:S(2)}) copy-start(f32[2,32,32,64]{3,2,1,0:T(8,128)S(1)} %reshape.613) | copy-start | bytes 1572868
  228.6 163.6 %copy-start.5 = (f32[1,2,65536]{2,1,0:T(2,128)S(1)}, f32[1,2,65536]{2,1,0:T(2,128)}, u32[]{:S(2)}) copy-start(f32[1,2,65536]{2,1,0:T(2,128)} %get-tuple-element.40) | copy-start | bytes 1572868
  228.6 163.6 %copy-start.6 = (f32[1,2,65536]{2,1,0:T(2,128)S(1)}, f32[1,2,65536]{2,1,0:T(2,128)}, u32[]{:S(2)}) copy-start(f32[1,2,65536]{2,1,0:T(2,128)} %get-tuple-element.41) | copy-start | bytes 1572868
  383.4 164.0 %all-to-all-start.4 = ((f32[64,1,4096]{2,1,0:T(1,128)}), f32[64,1,4096]{2,1,0:T(1,128)S(1)}, u32[]{:S(2)}, u32[]{:S(2)}) async-start(f32[64,1,4096]{2,1,0:T(1,128)} %reshape.642), calls=%async_computation.4 | async-start | bytes 2097152 | tf_op jit(solution)/shard_map/all_to_all | solution.py:177
  547.5 370.1 %all-to-all-start.8 = ((f32[64,1,4096]{2,1,0:T(1,128)}), f32[64,1,4096]{2,1,0:T(1,128)S(1)}, u32[]{:S(2)}, u32[]{:S(2)}) async-start(f32[64,1,4096]{2,1,0:T(1,128)} %reshape.648), calls=%async_computation.8 | async-start | bytes 2097152 | tf_op jit(solution)/shard_map/all_to_all | solution.py:180
  917.6 218.2 %all-to-all-start.10 = ((f32[64,1,4096]{2,1,0:T(1,128)}), f32[64,1,4096]{2,1,0:T(1,128)S(1)}, u32[]{:S(2)}, u32[]{:S(2)}) async-start(f32[64,1,4096]{2,1,0:T(1,128)} %reshape.652), calls=%async_computation.10 | async-start | bytes 2097152 | tf_op jit(solution)/shard_map/all_to_all | solution.py:183
  1135.7 214.1 %all-to-all-start.5 = ((bf16[64,2,512]{2,1,0:T(2,128)(2,1)}), bf16[64,2,512]{2,1,0:T(2,128)(2,1)S(1)}, u32[]{:S(2)}, u32[]{:S(2)}) async-start(bf16[64,2,512]{2,1,0:T(2,128)(2,1)} %reshape.644), calls=%async_computation.5 | async-start | bytes 262144 | tf_op jit(solution)/shard_map/all_to_all | solution.py:191
  1148.4 233.3 %copy-start.4 = (f32[1024,64]{0,1:T(8,128)S(1)}, f32[1024,64]{0,1:T(8,128)}, u32[]{:S(2)}) copy-start(f32[1024,64]{0,1:T(8,128)} %copy-done.3) | copy-start | bytes 786436
  1148.4 233.3 %copy-start.13 = (f32[1024]{0:T(1024)S(1)}, f32[1024]{0:T(1024)}, u32[]{:S(2)}) copy-start(f32[1024]{0:T(1024)} %copy-done.12) | copy-start | bytes 12292
  1148.4 233.3 %copy-start.15 = (f32[64]{0:T(128)S(1)}, f32[64]{0:T(128)}, u32[]{:S(2)}) copy-start(f32[64]{0:T(128)} %copy-done.14) | copy-start | bytes 772
  1148.4 233.3 %copy-start.17 = (f32[64]{0:T(128)S(1)}, f32[64]{0:T(128)}, u32[]{:S(2)}) copy-start(f32[64]{0:T(128)} %copy-done.16) | copy-start | bytes 772
  1148.4 233.8 %copy-start.7 = (f32[1024,64]{0,1:T(8,128)S(1)}, f32[1024,64]{0,1:T(8,128)}, u32[]{:S(2)}) copy-start(f32[1024,64]{0,1:T(8,128)} %get-tuple-element.71) | copy-start | bytes 786436
  1148.4 235.1 %copy-start.9 = (f32[1024,16]{0,1:T(8,128)S(1)}, f32[1024,16]{0,1:T(8,128)}, u32[]{:S(2)}) copy-start(f32[1024,16]{0,1:T(8,128)} %copy-done.8) | copy-start | bytes 196612
  1148.4 235.1 %copy-start.11 = (f32[1024,16]{0,1:T(8,128)S(1)}, f32[1024,16]{0,1:T(8,128)}, u32[]{:S(2)}) copy-start(f32[1024,16]{0,1:T(8,128)} %copy-done.10) | copy-start | bytes 196612
  1349.8 17.5 %all-to-all-start.9 = ((bf16[64,2,512]{2,1,0:T(2,128)(2,1)}), bf16[64,2,512]{2,1,0:T(2,128)(2,1)S(1)}, u32[]{:S(2)}, u32[]{:S(2)}) async-start(bf16[64,2,512]{2,1,0:T(2,128)(2,1)} %reshape.650), calls=%async_computation.9 | async-start | bytes 262144 | tf_op jit(solution)/shard_map/all_to_all | solution.py:198
  1367.4 13.2 all-to-all-start.11
where the time goes:
time: 1690 us; the launch traced here: 1670 us
  local copies, waits for them, and re-layouts  1130 us (67%)
  blocking collectives  288 us (17%)
  matrix products  88.8 us (5%)
  starting transfers between devices  88.6 us (5%)
  waiting for transfers between devices  44.2 us (3%)
  other arithmetic  33.8 us (2%)
    unnamed x52, local copies, waits for them, and re-layouts  683 us
    psum x1, blocking collectives, local(): lax.psum((out_part, embed_part, bias_part), 'seq')  276 us
    another operation x3, local copies, waits for them, and re-layouts, local_inverse(): return jnp.stack([final_r, final_i]).reshape(2, 2, seg_len * channels)  174 us
    all_to_all x2, local copies, waits for them, and re-layouts, local(): lax.all_to_all(local_inverse(prod_r, prod_i), 'seq', split_axis=2, concat...  71.5 us
    all_to_all x1, local copies, waits for them, and re-layouts, local(): lax.all_to_all(local_inverse(corr_r, corr_i), 'seq', split_axis=2, concat...  71 us
    all_to_all x1, local copies, waits for them, and re-layouts, local(): lax.all_to_all(local_inverse(grad_r, grad_i), 'seq', split_axis=2, concat...  71 us
    dot_general x24, matrix products, inner_dot(): jnp.einsum('eb,cdbh->cdeh', table, values, preferred_element_type=jnp.flo...  45 us
  transfers between devices with their start and end apart: 12, of which 6 were waited for; matrix products, arithmetic and copies ran while one was open for 59% of the time, Pallas kernels for 0%

commit v1 on v0

--- a/solution.py
+++ b/solution.py
@@ -174,8 +174,14 @@
     corr_r = cot_r * sig_r + cot_i * sig_i
     corr_i = cot_i * sig_r - cot_r * sig_i
     prod_back, grad_back, corr_back = (
-        lax.all_to_all(
-            local_inverse(prod_r, prod_i), "seq", split_axis=2, concat_axis=1, tiled=True
+        jnp.concatenate(
+            lax.all_to_all(
+                jnp.stack(jnp.split(local_inverse(prod_r, prod_i), lax.axis_size("seq"), axis=2)),
+                "seq",
+                0,
+                0,
+            ),
+            axis=1,
         ),
         lax.all_to_all(
             local_inverse(grad_r, grad_i), "seq", split_axis=2, concat_axis=1, tiled=True

time: 1690 us -> 1370 us (0.81)
  local copies, waits for them, and re-layouts: 1130 us -> 775 us
  other arithmetic: 33.8 us -> 68.9 us
    unnamed x52 -> x50, local copies, waits for them, and re-layouts: 683 us -> 457 us
    all_to_all x2 -> x0, local copies, waits for them, and re-layouts: 71.5 us -> none  [local(): lax.all_to_all(local_inverse(prod_r, prod_i), 'seq', split_axis=2, concat...]
    another operation x3 -> x2, local copies, waits for them, and re-layouts: 174 us -> 116 us  [local_inverse(): return jnp.stack([final_r, final_i]).reshape(2, 2, seg_len * channels)]
    unnamed x0 -> x63, other arithmetic: none -> 38.2 us
    all_to_all x1 -> x2, local copies, waits for them, and re-layouts: 71 us -> 71.5 us  [local(): lax.all_to_all(local_inverse(grad_r, grad_i), 'seq', split_axis=2, concat...]
  transfers between devices with their start and end apart: 12 -> 12, of which waited for: 6 -> 6; matrix products, arithmetic and copies ran while one was open for 59% -> 58% of each run, Pallas kernels for 0% -> 0%
where the time goes in v1:
time: 1370 us; the launch traced here: 1360 us
  local copies, waits for them, and re-layouts  775 us (57%)
  blocking collectives  287 us (21%)
  starting transfers between devices  96.8 us (7%)
  matrix products  88.7 us (6%)
  other arithmetic  68.9 us (5%)
  waiting for transfers between devices  44 us (3%)
    unnamed x50, local copies, waits for them, and re-layouts  457 us
    psum x1, blocking collectives, local(): lax.psum((out_part, embed_part, bias_part), 'seq')  276 us
    another operation x2, local copies, waits for them, and re-layouts, local_inverse(): return jnp.stack([final_r, final_i]).reshape(2, 2, seg_len * channels)  116 us
    all_to_all x2, local copies, waits for them, and re-layouts, local(): lax.all_to_all(local_inverse(grad_r, grad_i), 'seq', split_axis=2, concat...  71.5 us
    all_to_all x1, local copies, waits for them, and re-layouts, local(): lax.all_to_all(local_inverse(corr_r, corr_i), 'seq', split_axis=2, concat...  71 us
    dot_general x24, matrix products, inner_dot(): jnp.einsum('eb,cdbh->cdeh', table, values, preferred_element_type=jnp.flo...  45 us
    unnamed x63, other arithmetic  38.2 us
    dot_general x24, matrix products, side_dot(): jnp.einsum('db,cbm->cdm', table, values, preferred_element_type=jnp.float...  29.2 us
  transfers between devices with their start and end apart: 12, of which 6 were waited for; matrix products, arithmetic and copies ran while one was open for 58% of the time, Pallas kernels for 0%

profile of v1, /device:TPU:0, one launch (start us, length us, event | category | flops | bytes accessed | tf_op | source)
XLA Modules:
  0.0 1363.3 jit_solution(13126591315604744971)
XLA Ops:
  4.5 9.9 all-to-all-start
  19.5 2.7 fusion.553
  24.7 8.8 all-to-all-start.6
  34.2 7.9 all-to-all-done.6
  42.1 4.9 all-to-all-start.2
  49.0 7.9 all-to-all-done.2
  59.6 3.0 multiply_add_fusion.8
  65.2 1.9 pad_maximum_fusion.1
  67.2 4.7 all-to-all-start.3
  79.7 2.0 pad_maximum_fusion.2
  81.7 3.0 pad_maximum_fusion
  84.7 5.2 all-to-all-done.3
  89.9 4.7 all-to-all-start.1
  94.6 1.6 fusion.550
  101.6 11.2 all-to-all-done.1
  112.7 14.3 %all-to-all-start.7 = ((f32[2,128,1024]{2,0,1:T(2,128)}), f32[2,128,1024]{2,0,1:T(2,128)}, u32[]{:S(2)}, u32[]{:S(2)}) async-start(f32[2,128,1024]{2,0,1:T(2,128)} %pad_maximum_fusion.2), calls=%async_computation.7 | async-start | bytes 2097152 | tf_op jit(solution)/shard_map/all_to_all | solution.py:158
  132.0 2.2 fusion.40
  134.3 2.5 fusion.3
  138.2 2.8 reshape.616
  141.0 2.3 fusion.39
  143.3 3.5 fusion.42
  146.8 3.5 fusion.41
  150.2 3.8 fusion.548
  155.0 2.0 squeeze.48
  157.0 2.5 fusion.196
  159.6 2.0 copy.92
  161.6 2.1 squeeze.49
  163.6 1.7 fusion.194
  165.3 2.7 fusion.6
  168.0 2.6 fusion.7
  176.1 2.8 convolution_subtract_fusion.11
  178.9 2.8 convolution_add_fusion.11
  181.7 3.1 convolution_subtract_fusion.10
  184.9 3.6 convolution_add_fusion.10
  189.8 1.9 multiply_add_fusion
  204.0 3.2 subtract_bitcast_fusion
  207.2 1.6 reshape.632
  209.1 1.6 reshape.628
  211.1 1.6 reshape.619
  212.7 1.6 reshape.618
  220.0 1.5 reshape.620
  230.8 1.9 reshape.635
  232.7 3.7 multiply_subtract_fusion.6
  275.2 8.8 all-to-all-start.4
  284.5 57.8 %copy.93 = f32[2,2,65536]{1,0,2:T(2,128)} copy(f32[2,2,65536]{2,1,0:T(2,128)S(1)} %pad_maximum_fusion.3) | data formatting | bytes 2097152 | tf_op jit(solution)/shard_map/stack | solution.py:122
  342.3 96.8 %reshape.651 = f32[64,1,4096]{2,1,0:T(1,128)} reshape(f32[65536,2,2]{2,1,0:T(2,128)} %bitcast.388) | data formatting | bytes 2097152
  439.0 8.8 all-to-all-start.8
  447.9 1.7 pad_maximum_fusion.4
  449.6 57.8 %copy.96 = f32[2,2,65536]{1,0,2:T(2,128)} copy(f32[2,2,65536]{2,1,0:T(2,128)S(1)} %pad_maximum_fusion.4) | data formatting | bytes 2097152 | tf_op jit(solution)/shard_map/stack | solution.py:122
  507.4 96.8 %reshape.655 = f32[64,1,4096]{2,1,0:T(1,128)} reshape(f32[65536,2,2]{2,1,0:T(2,128)} %bitcast.390) | data formatting | bytes 2097152
  606.8 9.0 all-to-all-start.10
  618.9 3.3 reduce.7
  622.1 129.1 %reshape.652 = f32[65536,2,2]{2,1,0:T(2,128)} reshape(f32[64,4096]{1,0:T(8,128)S(1)} %reduce.7) | data formatting | bytes 2097152
  751.3 71.0 %copy.94 = f32[2,2,64,1024]{3,1,2,0:T(2,128)S(1)} copy(f32[2,2,64,1024]{1,0,3,2:T(2,128)} %bitcast.117) | data formatting | bytes 2097152 | tf_op jit(solution)/shard_map/all_to_all | solution.py:186
  825.6 9.2 all-to-all-start.5
  834.8 3.3 reduce.9
  838.1 129.1 %reshape.656 = f32[65536,2,2]{2,1,0:T(2,128)} reshape(f32[64,4096]{1,0:T(8,128)S(1)} %reduce.9) | data formatting | bytes 2097152
  967.2 71.0 %copy.97 = f32[2,2,64,1024]{3,1,2,0:T(2,128)S(1)} copy(f32[2,2,64,1024]{1,0,3,2:T(2,128)} %bitcast.126) | data formatting | bytes 2097152 | tf_op jit(solution)/shard_map/all_to_all | solution.py:189
  1039.6 9.2 all-to-all-start.9
  1050.7 6.3 all-to-all-done.9
  1057.1 4.6 all-to-all-start.11
  1064.8 5.4 all-to-all-done.11
  1073.6 276.3 %all-reduce = (f32[32,64]{1,0:T(8,128)S(1)}, f32[64]{0:T(128)S(1)}, f32[64,64]{1,0:T(8,128)S(1)}) all-reduce(f32[32,64]{1,0:T(8,128)S(1)} %fusion.61, f32[64]{0:T(128)S(1)} %get-tuple-element.72, f32[64,64]{1,0:T(8,128)S(1)} %fusion.48), channel_id=1, replica_groups=mesh['seq'=64,'chan'=2] {'seq'}, use_global_device_ids=true, to_apply=%region_0.1 | all-reduce | flops 6208 | bytes 49664 | tf_op jit(solution)/shard_map/psum | solution.py:226
  1350.0 11.2 all-reduce.1
  (242 shorter events, 134.1 us)
Async XLA Ops:
  0.6 22.3 %copy-start = (f32[64,64]{1,0:T(8,128)S(1)}, f32[64,64]{1,0:T(8,128)}, u32[]{:S(2)}) copy-start(f32[64,64]{1,0:T(8,128)} %param.12) | copy-start | bytes 49156
  4.5 20.2 %all-to-all-start = ((bf16[64,2,512]{2,1,0:T(2,128)(2,1)}), bf16[64,2,512]{2,1,0:T(2,128)(2,1)S(1)}, u32[]{:S(2)}, u32[]{:S(2)}) async-start(bf16[64,2,512]{2,1,0:T(2,128)(2,1)} %reshape.645), calls=%async_computation | async-start | bytes 262144 | tf_op jit(solution)/shard_map/all_to_all | solution.py:128
  14.4 7.8 copy-start.12
  15.1 7.1 copy-start.14
  15.1 7.1 copy-start.16
  19.5 2.7 copy-start.8
  19.5 2.7 copy-start.10
  22.2 0.7 copy-start.3
  24.7 17.4 %all-to-all-start.6 = ((bf16[64,2,512]{2,1,0:T(2,128)(2,1)}), bf16[64,2,512]{2,1,0:T(2,128)(2,1)S(1)}, u32[]{:S(2)}, u32[]{:S(2)}) async-start(bf16[64,2,512]{2,1,0:T(2,128)(2,1)} %reshape.649), calls=%async_computation.6 | async-start | bytes 262144 | tf_op jit(solution)/shard_map/all_to_all | solution.py:135
  42.1 14.8 %all-to-all-start.2 = ((f32[64,1,1024]{2,1,0:T(1,128)}), f32[64,1,1024]{2,1,0:T(1,128)S(1)}, u32[]{:S(2)}, u32[]{:S(2)}) async-start(f32[64,1,1024]{2,1,0:T(1,128)} %all_to_all.132), calls=%async_computation.2 | async-start | bytes 524288 | tf_op jit(solution)/shard_map/all_to_all | solution.py:147
  67.2 22.7 %all-to-all-start.3 = ((f32[2,128,1024]{2,0,1:T(2,128)}), f32[2,128,1024]{2,0,1:T(2,128)S(1)}, u32[]{:S(2)}, u32[]{:S(2)}) async-start(f32[2,128,1024]{2,0,1:T(2,128)} %pad_maximum_fusion.1), calls=%async_computation.3 | async-start | bytes 2097152 | tf_op jit(solution)/shard_map/all_to_all | solution.py:165
  89.9 22.8 %all-to-all-start.1 = ((f32[2,128,1024]{2,0,1:T(2,128)}), f32[2,128,1024]{2,0,1:T(2,128)S(1)}, u32[]{:S(2)}, u32[]{:S(2)}) async-start(f32[2,128,1024]{2,0,1:T(2,128)} %pad_maximum_fusion), calls=%async_computation.1 | async-start | bytes 2097152 | tf_op jit(solution)/shard_map/all_to_all | solution.py:151
  112.7 37.5 %all-to-all-start.7 = ((f32[2,128,1024]{2,0,1:T(2,128)}), f32[2,128,1024]{2,0,1:T(2,128)}, u32[]{:S(2)}, u32[]{:S(2)}) async-start(f32[2,128,1024]{2,0,1:T(2,128)} %pad_maximum_fusion.2), calls=%async_computation.7 | async-start | bytes 2097152 | tf_op jit(solution)/shard_map/all_to_all | solution.py:158
  132.0 36.0 %copy-start.1 = (f32[2,32,32,64]{3,2,1,0:T(8,128)}, f32[2,32,32,64]{3,2,1,0:T(8,128)S(1)}, u32[]{:S(2)}) copy-start(f32[2,32,32,64]{3,2,1,0:T(8,128)S(1)} %reshape.614) | copy-start | bytes 1572868
  138.2 32.4 %copy-start.2 = (f32[2,32,32,64]{3,2,1,0:T(8,128)}, f32[2,32,32,64]{3,2,1,0:T(8,128)S(1)}, u32[]{:S(2)}) copy-start(f32[2,32,32,64]{3,2,1,0:T(8,128)S(1)} %reshape.617) | copy-start | bytes 1572868
  236.3 47.6 %copy-start.5 = (f32[1,2,65536]{2,1,0:T(2,128)S(1)}, f32[1,2,65536]{2,1,0:T(2,128)}, u32[]{:S(2)}) copy-start(f32[1,2,65536]{2,1,0:T(2,128)} %get-tuple-element.40) | copy-start | bytes 1572868
  236.4 47.6 %copy-start.6 = (f32[1,2,65536]{2,1,0:T(2,128)S(1)}, f32[1,2,65536]{2,1,0:T(2,128)}, u32[]{:S(2)}) copy-start(f32[1,2,65536]{2,1,0:T(2,128)} %get-tuple-element.41) | copy-start | bytes 1572868
  275.2 163.8 %all-to-all-start.4 = ((f32[64,2,2,1024]{3,2,1,0:T(2,128)}), f32[64,2,2,1024]{3,2,1,0:T(2,128)S(1)}, u32[]{:S(2)}, u32[]{:S(2)}) async-start(f32[64,2,2,1024]{3,2,1,0:T(2,128)} %constant_dynamic-update-slice_fusion), calls=%async_computation.4 | async-start | bytes 2097152 | tf_op jit(solution)/shard_map/all_to_all | solution.py:178
  439.0 167.8 %all-to-all-start.8 = ((f32[64,1,4096]{2,1,0:T(1,128)}), f32[64,1,4096]{2,1,0:T(1,128)S(1)}, u32[]{:S(2)}, u32[]{:S(2)}) async-start(f32[64,1,4096]{2,1,0:T(1,128)} %reshape.651), calls=%async_computation.8 | async-start | bytes 2097152 | tf_op jit(solution)/shard_map/all_to_all | solution.py:186
  606.8 218.7 %all-to-all-start.10 = ((f32[64,1,4096]{2,1,0:T(1,128)}), f32[64,1,4096]{2,1,0:T(1,128)S(1)}, u32[]{:S(2)}, u32[]{:S(2)}) async-start(f32[64,1,4096]{2,1,0:T(1,128)} %reshape.655), calls=%async_computation.10 | async-start | bytes 2097152 | tf_op jit(solution)/shard_map/all_to_all | solution.py:189
  825.6 214.0 %all-to-all-start.5 = ((bf16[64,2,512]{2,1,0:T(2,128)(2,1)}), bf16[64,2,512]{2,1,0:T(2,128)(2,1)S(1)}, u32[]{:S(2)}, u32[]{:S(2)}) async-start(bf16[64,2,512]{2,1,0:T(2,128)(2,1)} %reshape.647), calls=%async_computation.5 | async-start | bytes 262144 | tf_op jit(solution)/shard_map/all_to_all | solution.py:197
  838.0 233.4 %copy-start.4 = (f32[1024,64]{0,1:T(8,128)S(1)}, f32[1024,64]{0,1:T(8,128)}, u32[]{:S(2)}) copy-start(f32[1024,64]{0,1:T(8,128)} %copy-done.3) | copy-start | bytes 786436
  838.0 233.4 %copy-start.13 = (f32[1024]{0:T(1024)S(1)}, f32[1024]{0:T(1024)}, u32[]{:S(2)}) copy-start(f32[1024]{0:T(1024)} %copy-done.12) | copy-start | bytes 12292
  838.0 233.4 %copy-start.15 = (f32[64]{0:T(128)S(1)}, f32[64]{0:T(128)}, u32[]{:S(2)}) copy-start(f32[64]{0:T(128)} %copy-done.14) | copy-start | bytes 772
  838.1 233.4 %copy-start.17 = (f32[64]{0:T(128)S(1)}, f32[64]{0:T(128)}, u32[]{:S(2)}) copy-start(f32[64]{0:T(128)} %copy-done.16) | copy-start | bytes 772
  838.1 233.9 %copy-start.7 = (f32[1024,64]{0,1:T(8,128)S(1)}, f32[1024,64]{0,1:T(8,128)}, u32[]{:S(2)}) copy-start(f32[1024,64]{0,1:T(8,128)} %get-tuple-element.71) | copy-start | bytes 786436
  838.1 235.2 %copy-start.9 = (f32[1024,16]{0,1:T(8,128)S(1)}, f32[1024,16]{0,1:T(8,128)}, u32[]{:S(2)}) copy-start(f32[1024,16]{0,1:T(8,128)} %copy-done.8) | copy-start | bytes 196612
  838.1 235.2 %copy-start.11 = (f32[1024,16]{0,1:T(8,128)S(1)}, f32[1024,16]{0,1:T(8,128)}, u32[]{:S(2)}) copy-start(f32[1024,16]{0,1:T(8,128)} %copy-done.10) | copy-start | bytes 196612
  1039.6 17.5 %all-to-all-start.9 = ((bf16[64,2,512]{2,1,0:T(2,128)(2,1)}), bf16[64,2,512]{2,1,0:T(2,128)(2,1)S(1)}, u32[]{:S(2)}, u32[]{:S(2)}) async-start(bf16[64,2,512]{2,1,0:T(2,128)(2,1)} %reshape.653), calls=%async_computation.9 | async-start | bytes 262144 | tf_op jit(solution)/shard_map/all_to_all | solution.py:204
  1057.1 13.2 all-to-all-start.11
